TPU v7x, 512 devices: a whole 4x4x16 slice. The times are simulated.
512 devices in a mesh: head: 8 (over x, core), expert: 64 (over z, y).
Axes of the slice: x: 4, y: 4, z: 16, core: 2. Of those that a mesh axis runs over, the one named last changes fastest.
Arguments:
- q_latent: bfloat16 [512, 64, 512], P('expert', 'head'), may hold values from -16 to 16
- q_rotary: bfloat16 [512, 64, 64], P('expert', 'head'), may hold values from -3 to 3
- cache_latent: bfloat16 [512, 128, 512], P('expert'), may hold values from -5 to 5
- cache_rotary: bfloat16 [512, 64, 128], P('expert'), may hold values from -5 to 5
- lengths: int32 [512], P('expert'), may hold values from 16 to 128, as said below
- w_value_out: bfloat16 [32768, 5120], P('head', 'expert'), may hold values from -0.25 to 0.25
- resid: bfloat16 [512, 5120], P('expert'), may hold values from -8 to 8
- norm_gain: float32 [5120], replicated, may hold values from 0.1 to 1.9
- route_ids: int32 [512, 6], P('expert'), may hold values from 0 to 63, as said below
- route_weights: float32 [512, 6], P('expert'), may hold values from 0.1 to 0.6
- w_gate_up: bfloat16 [64, 2, 768, 5120], P('expert', None, 'head'), may hold values from -0.078125 to 0.078125
- w_down: bfloat16 [64, 768, 5120], P('expert', 'head'), may hold values from -0.21875 to 0.21875
Outputs:
- mixed_out: float32 [512, 5120], P('expert', 'head')
Inputs may be any that keep to these rules, and one draw needn't show every extreme that they name: `lengths`: slots at positions below a sequence's length are valid; some sequence has length 128. `route_ids`: each row names 6 different experts. Among the rows of one device (aligned blocks of 8 rows) no expert is named by more than 2 rows, and one expert is named by exactly 2 rows in every block.
All inputs are finite; a program needn't handle non-finite values.
Results may differ from a plain program's by a relative error of at most 0.0046.
Values may be sent and summed in bfloat16 or wider, within the bound.
No kernel may reach another device: no remote copies, remote signals or barrier semaphores. Data moves between devices by JAX's collectives and lax.ppermute only.
A program may use at most 64 MiB of HBM per device.

v0:
```python
import jax
import jax.numpy as jnp
from jax import lax
from jax.sharding import Mesh
from jax.sharding import PartitionSpec as P

EXPERT = ("ez", "ey")
softmax_scale = 192.0 ** (-0.5)
norm_epsilon = 1e-06


def attend(q_latent, q_rotary, cache_latent, cache_rotary, lengths):
    scores = jnp.einsum("shl,scl->shc", q_latent, cache_latent, preferred_element_type=jnp.float32)
    scores = scores + jnp.einsum(
        "shr,src->shc", q_rotary, cache_rotary, preferred_element_type=jnp.float32
    )
    scores = scores * softmax_scale
    position = lax.broadcasted_iota(jnp.int32, scores.shape, 2)
    scores = jnp.where(position < lengths[:, None, None], scores, -1e30)
    highest = jnp.max(scores, axis=2, keepdims=True)
    weights = jnp.exp(scores - highest)
    probs = (weights / jnp.sum(weights, axis=2, keepdims=True)).astype(jnp.bfloat16)
    return jnp.einsum(
        "shc,scl->shl", probs, cache_latent, preferred_element_type=jnp.float32
    ).astype(jnp.bfloat16)


def on_device(
    q_latent,
    q_rotary,
    cache_latent,
    cache_rotary,
    lengths,
    w_value_out,
    resid,
    norm_gain,
    route_ids,
    route_weights,
    w_gate_up,
    w_down,
):
    seq_local = q_latent.shape[0]
    latent_out = attend(q_latent, q_rotary, cache_latent, cache_rotary, lengths)
    flattened = latent_out.reshape(seq_local, -1)
    z_count = lax.axis_size("ez")
    latent_copies = jnp.broadcast_to(flattened[None], (z_count,) + flattened.shape)
    gathered = lax.all_to_all(latent_copies, "ez", split_axis=0, concat_axis=0, tiled=True)
    gathered = gathered.reshape(-1, flattened.shape[1])
    value_blocks = lax.all_gather(w_value_out, "ey", axis=0, tiled=False)
    column_terms = jnp.einsum(
        "sk,jkc->sjc", gathered, value_blocks, preferred_element_type=jnp.float32
    ).reshape(gathered.shape[0], -1)
    column_sums = lax.psum(column_terms, "head")
    attention = lax.all_to_all(
        column_sums.astype(jnp.bfloat16), "ez", split_axis=0, concat_axis=1, tiled=True
    )
    stream = resid.astype(jnp.float32) + attention.astype(jnp.float32)
    mean_square = jnp.mean(stream * stream, axis=1, keepdims=True)
    normed = (stream * lax.rsqrt(mean_square + norm_epsilon) * norm_gain).astype(jnp.bfloat16)
    expert_count = lax.axis_size("ez") * lax.axis_size("ey")
    top_count = route_ids.shape[1]
    capacity = max(2, -(-(seq_local * top_count) // expert_count))
    flat_ids = route_ids.reshape(-1)
    one_hot = (flat_ids[:, None] == jnp.arange(expert_count, dtype=jnp.int32)[None, :]).astype(
        jnp.int32
    )
    earlier = jnp.cumsum(one_hot, axis=0) - one_hot
    slot_index = jnp.sum(earlier * one_hot, axis=1)
    target = (flat_ids * capacity + slot_index).reshape(seq_local, top_count)
    places = jnp.arange(expert_count * capacity, dtype=jnp.int32)
    matches = target[None, :, :] == places[:, None, None]
    selector = jnp.sum(matches.astype(jnp.int32), axis=2).astype(jnp.bfloat16)
    blending = jnp.sum(jnp.where(matches, route_weights[None, :, :], 0.0), axis=2)
    gate_up = w_gate_up[0]
    col_width = stream.shape[1] // lax.axis_size("head")
    offset = lax.axis_index("head") * col_width
    normed_cols = lax.dynamic_slice_in_dim(normed, offset, col_width, 1)
    outgoing = jnp.dot(selector, normed_cols, preferred_element_type=jnp.float32).astype(
        jnp.bfloat16
    )
    outgoing = outgoing.reshape(expert_count, capacity, -1)
    arrived = lax.all_to_all(outgoing, EXPERT, split_axis=0, concat_axis=0, tiled=True)
    arrived_cols = arrived.reshape(-1, arrived.shape[2])
    head_count = lax.axis_size("head")
    down_blocks = w_down[0].reshape(w_down.shape[1], head_count, -1)
    arrived_cols, down_blocks = lax.optimization_barrier((arrived_cols, down_blocks))
    down_cols = lax.all_to_all(down_blocks, "head", split_axis=1, concat_axis=0, tiled=True)
    down_cols = down_cols.reshape(-1, down_blocks.shape[2])
    flat_rows = lax.all_gather(arrived_cols, "head", axis=1, tiled=True)
    projected = jnp.einsum("rd,gfd->rgf", flat_rows, gate_up, preferred_element_type=jnp.float32)
    hidden = (jax.nn.silu(projected[:, 0]) * projected[:, 1]).astype(jnp.bfloat16)
    hidden_all = lax.all_gather(hidden, "head", axis=1, tiled=True)
    summed_cols = jnp.dot(hidden_all, down_cols, preferred_element_type=jnp.float32).astype(
        jnp.bfloat16
    )
    summed_rows = summed_cols.reshape(expert_count, capacity, -1)
    returned = lax.all_to_all(summed_rows, EXPERT, split_axis=0, concat_axis=0, tiled=True)
    back_rows = returned.reshape(expert_count * capacity, -1).astype(jnp.float32)
    mixture = jnp.dot(blending.T, back_rows, precision=lax.Precision.HIGHEST)
    stream_cols = lax.dynamic_slice_in_dim(stream, offset, col_width, 1)
    return stream_cols + mixture


def solution(mesh):
    placed = (
        P(EXPERT, "head", None),
        P(EXPERT, "head", None),
        P(EXPERT, None, None),
        P(EXPERT, None, None),
        P(EXPERT),
        P("head", EXPERT),
        P(EXPERT, None),
        P(),
        P(EXPERT, None),
        P(EXPERT, None),
        P(EXPERT, None, "head", None),
        P(EXPERT, "head", None),
    )
    head_count, expert_total = mesh.devices.shape
    y_count = len({device.coords[1] for device in mesh.devices[0]})
    split_mesh = Mesh(
        mesh.devices.reshape(head_count, expert_total // y_count, y_count), ("head",) + EXPERT
    )
    return jax.shard_map(
        on_device, mesh=split_mesh, in_specs=placed, out_specs=P(EXPERT, "head"), check_vma=False
    )
```

profile of v0, /device:TPU:8, one launch (start us, length us, event | category | flops | bytes accessed | tf_op | source)
XLA Modules:
  0.0 234.2 jit_solution(10736050746131402408)
XLA Ops:
  6.5 0.7 all-gather.6.cloned.1.call-update
  7.3 1.6 fusion.20
  8.9 1.1 fusion.8
  10.1 0.3 fusion.4
  10.5 1.1 broadcast_in_dim.33
  11.6 15.2 %all-to-all-start = ((bf16[16,8,4096]{2,1,0:T(8,128)(2,1)}), bf16[16,8,4096]{2,1,0:T(8,128)(2,1)S(1)}, u32[]{:S(2)}, u32[]{:S(2)}) async-start(bf16[16,8,4096]{2,1,0:T(8,128)(2,1)} %broadcast_in_dim.33), calls=%async_computation | async-start | bytes 2097152 | tf_op jit(solution)/shard_map/all_to_all | solution.py:47
  27.3 28.6 %all-gather.6.cloned.1.call-done = bf16[16384,80]{0,1:T(8,128)(2,1)} async-done(((bf16[4096,80]{0,1:T(8,128)(2,1)}), bf16[16384,80]{0,1:T(8,128)(2,1)}) %all-gather.6.cloned.1.call-update) | async-done | bytes 2621456 | tf_op jit(solution)/shard_map/all_gather | solution.py:49
  55.9 5.5 %reshape.55 = bf16[4,4096,80]{1,0,2:T(4,128)(2,1)} reshape(bf16[16384,80]{0,1:T(8,128)(2,1)} %all-gather.6.cloned.1.call-done) | data formatting | bytes 5242880 | tf_op jit(solution)/shard_map/all_gather | solution.py:49
  61.4 4.7 %copy.24 = bf16[4,80,4096]{2,1,0:T(8,128)(2,1)} copy(bf16[4,80,4096]{2,0,1:T(4,128)(2,1)} %bitcast.50) | data formatting | bytes 5242880 | tf_op jit(solution)/shard_map/sk,jkc->sjc/dot_general | solution.py:50
  66.1 10.7 %all-to-all-done = bf16[16,8,4096]{2,1,0:T(8,128)(2,1)S(1)} async-done(((bf16[16,8,4096]{2,1,0:T(8,128)(2,1)}), bf16[16,8,4096]{2,1,0:T(8,128)(2,1)S(1)}, u32[]{:S(2)}, u32[]{:S(2)}) %all-to-all-start) | async-done | bytes 1048608 | tf_op jit(solution)/shard_map/all_to_all | solution.py:47
  76.8 2.6 %fusion.9 = f32[128,320]{0,1:T(8,128)S(1)} fusion(bf16[320,4096]{1,0:T(8,128)(2,1)} %bitcast.49, bf16[16,8,4096]{2,1,0:T(8,128)(2,1)S(1)} %all-to-all-done), kind=kOutput, calls=%fused_computation.14 | convolution fusion | flops 335544320 | bytes 3833856 | tf_op jit(solution)/shard_map/sk,jkc->sjc/dot_general | solution.py:50
  79.4 25.1 %all-reduce.1 = bf16[128,320]{0,1:T(8,128)(2,1)S(1)} all-reduce(f32[128,320]{0,1:T(8,128)S(1)} %fusion.9), channel_id=1, replica_groups=mesh['head'=8,'ez'=16,'ey'=4] {'head'}, use_global_device_ids=true, to_apply=%region_2.3 | all-reduce | flops 40960 | bytes 245760 | tf_op jit(solution)/shard_map/psum | solution.py:53
  104.5 0.7 copy.25
  105.2 10.2 %all-to-all-start.1 = ((bf16[16,8,320]{2,1,0:T(8,128)(2,1)}), bf16[16,8,320]{2,1,0:T(8,128)(2,1)S(1)}, u32[]{:S(2)}, u32[]{:S(2)}) async-start(bf16[16,8,320]{2,1,0:T(8,128)(2,1)} %bitcast.3), calls=%async_computation.1 | async-start | bytes 196608 | tf_op jit(solution)/shard_map/all_to_all | solution.py:54
  115.6 0.8 dynamic-slice
  116.4 12.1 %all-to-all-done.1 = bf16[16,8,320]{2,1,0:T(8,128)(2,1)S(1)} async-done(((bf16[16,8,320]{2,1,0:T(8,128)(2,1)}), bf16[16,8,320]{2,1,0:T(8,128)(2,1)S(1)}, u32[]{:S(2)}, u32[]{:S(2)}) %all-to-all-start.1) | async-done | bytes 81952 | tf_op jit(solution)/shard_map/all_to_all | solution.py:54
  128.8 0.3 convolution_convert_fusion.1
  129.1 0.7 reshape.49
  129.9 7.0 %all-to-all-start.2 = ((bf16[64,2,640]{2,1,0:T(2,128)(2,1)}), bf16[64,2,640]{2,1,0:T(2,128)(2,1)S(1)}, u32[]{:S(2)}, u32[]{:S(2)}) async-start(bf16[64,2,640]{2,1,0:T(2,128)(2,1)} %reshape.49), calls=%async_computation.2 | async-start | bytes 327680 | tf_op jit(solution)/shard_map/all_to_all | solution.py:82
  136.9 1.3 copy.31
  138.2 14.4 %all-to-all-done.2 = bf16[64,2,640]{2,1,0:T(2,128)(2,1)S(1)} async-done(((bf16[64,2,640]{2,1,0:T(2,128)(2,1)}), bf16[64,2,640]{2,1,0:T(2,128)(2,1)S(1)}, u32[]{:S(2)}, u32[]{:S(2)}) %all-to-all-start.2) | async-done | bytes 163872 | tf_op jit(solution)/shard_map/all_to_all | solution.py:82
  152.6 0.7 reshape.50
  153.3 1.1 copy.29
  154.4 5.0 %all-to-all-start.3 = ((bf16[96,8,640]{2,0,1:T(8,128)(2,1)}), bf16[96,8,640]{2,0,1:T(8,128)(2,1)S(1)}, u32[]{:S(2)}, u32[]{:S(2)}) async-start(bf16[96,8,640]{2,0,1:T(8,128)(2,1)} %copy.29), calls=%async_computation.3 | async-start | bytes 1966080 | tf_op jit(solution)/shard_map/all_to_all | solution.py:87
  159.4 19.3 %all-gather.4.cloned.1.call-done = bf16[128,5120]{1,0:T(8,128)(2,1)} async-done(((bf16[128,640]{1,0:T(8,128)(2,1)}), bf16[128,5120]{1,0:T(8,128)(2,1)}) %all-gather.4.cloned.1.call-update) | async-done | bytes 1310736 | tf_op jit(solution)/shard_map/all_gather | solution.py:89
  178.7 2.0 fusion.1
  180.8 12.8 %all_gather.15 = bf16[128,768]{0,1:T(8,128)(2,1)S(1)} all-gather(bf16[128,96]{0,1:T(8,128)(2,1)S(1)} %fusion.12), channel_id=1, replica_groups=mesh['head'=8,'ez'=16,'ey'=4] {'head'}, dimensions={1}, use_global_device_ids=true | all-gather | bytes 221184 | tf_op jit(solution)/shard_map/all_gather | solution.py:92
  193.6 0.3 convolution_convert_fusion
  193.9 0.7 reshape.52
  194.6 13.5 %all-to-all-start.4 = ((bf16[64,2,640]{2,1,0:T(2,128)(2,1)}), bf16[64,2,640]{2,1,0:T(2,128)(2,1)S(1)}, u32[]{:S(2)}, u32[]{:S(2)}) async-start(bf16[64,2,640]{2,1,0:T(2,128)(2,1)} %reshape.52), calls=%async_computation.4 | async-start | bytes 327680 | tf_op jit(solution)/shard_map/all_to_all | solution.py:97
  208.3 18.2 %all-to-all-done.4 = bf16[64,2,640]{2,1,0:T(2,128)(2,1)S(1)} async-done(((bf16[64,2,640]{2,1,0:T(2,128)(2,1)}), bf16[64,2,640]{2,1,0:T(2,128)(2,1)S(1)}, u32[]{:S(2)}, u32[]{:S(2)}) %all-to-all-start.4) | async-done | bytes 163872 | tf_op jit(solution)/shard_map/all_to_all | solution.py:97
  226.6 0.8 convolution_add_fusion.1
  (33 shorter events, 1.5 us)
Async XLA Ops:
  6.5 172.2 %copy-start = (bf16[1,2,96,5120]{3,2,1,0:T(8,128)(2,1)S(1)}, bf16[1,2,96,5120]{3,2,1,0:T(8,128)(2,1)}, u32[]{:S(2)}) copy-start(bf16[1,2,96,5120]{3,2,1,0:T(8,128)(2,1)} %param.22) | copy-start | bytes 5898244
  6.5 3.6 %copy-start.1 = (bf16[8,128,512]{2,1,0:T(8,128)(2,1)S(1)}, bf16[8,128,512]{2,1,0:T(8,128)(2,1)}, u32[]{:S(2)}) copy-start(bf16[8,128,512]{2,1,0:T(8,128)(2,1)} %param.14) | copy-start | bytes 3145732
  6.5 49.3 %all-gather.6.cloned.1.call-start = ((), (), s32[]{:S(2)}) async-start(), calls=%async_computation.6 | async-start | bytes 3276800 | tf_op jit(solution)/shard_map/all_gather | solution.py:49
  10.4 16.4 %copy-start.3 = (s32[8,6]{1,0:T(8,128)S(1)}, s32[8,6]{1,0:T(8,128)}, u32[]{:S(2)}) copy-start(s32[8,6]{1,0:T(8,128)} %param.20) | copy-start | bytes 580
  11.6 65.2 %all-to-all-start = ((bf16[16,8,4096]{2,1,0:T(8,128)(2,1)}), bf16[16,8,4096]{2,1,0:T(8,128)(2,1)S(1)}, u32[]{:S(2)}, u32[]{:S(2)}) async-start(bf16[16,8,4096]{2,1,0:T(8,128)(2,1)} %broadcast_in_dim.33), calls=%async_computation | async-start | bytes 2097152 | tf_op jit(solution)/shard_map/all_to_all | solution.py:47
  76.8 51.9 %copy-start.2 = (bf16[8,5120]{1,0:T(8,128)(2,1)S(1)}, bf16[8,5120]{1,0:T(8,128)(2,1)}, u32[]{:S(2)}) copy-start(bf16[8,5120]{1,0:T(8,128)(2,1)} %param.18) | copy-start | bytes 245764
  105.2 23.2 %all-to-all-start.1 = ((bf16[16,8,320]{2,1,0:T(8,128)(2,1)}), bf16[16,8,320]{2,1,0:T(8,128)(2,1)S(1)}, u32[]{:S(2)}, u32[]{:S(2)}) async-start(bf16[16,8,320]{2,1,0:T(8,128)(2,1)} %bitcast.3), calls=%async_computation.1 | async-start | bytes 196608 | tf_op jit(solution)/shard_map/all_to_all | solution.py:54
  129.9 22.7 %all-to-all-start.2 = ((bf16[64,2,640]{2,1,0:T(2,128)(2,1)}), bf16[64,2,640]{2,1,0:T(2,128)(2,1)S(1)}, u32[]{:S(2)}, u32[]{:S(2)}) async-start(bf16[64,2,640]{2,1,0:T(2,128)(2,1)} %reshape.49), calls=%async_computation.2 | async-start | bytes 327680 | tf_op jit(solution)/shard_map/all_to_all | solution.py:82
  136.8 41.9 %all-gather.4.cloned.1.call-start = ((), (), s32[]{:S(2)}) async-start(), calls=%async_computation.5 | async-start | bytes 1474560 | tf_op jit(solution)/shard_map/all_gather | solution.py:89
  154.4 39.1 %all-to-all-start.3 = ((bf16[96,8,640]{2,0,1:T(8,128)(2,1)}), bf16[96,8,640]{2,0,1:T(8,128)(2,1)S(1)}, u32[]{:S(2)}, u32[]{:S(2)}) async-start(bf16[96,8,640]{2,0,1:T(8,128)(2,1)} %copy.29), calls=%async_computation.3 | async-start | bytes 1966080 | tf_op jit(solution)/shard_map/all_to_all | solution.py:87
  180.7 27.4 %copy-start.4 = (f32[8,6]{1,0:T(8,128)S(1)}, f32[8,6]{1,0:T(8,128)}, u32[]{:S(2)}) copy-start(f32[8,6]{1,0:T(8,128)} %param.21) | copy-start | bytes 580
  194.6 31.9 %all-to-all-start.4 = ((bf16[64,2,640]{2,1,0:T(2,128)(2,1)}), bf16[64,2,640]{2,1,0:T(2,128)(2,1)S(1)}, u32[]{:S(2)}, u32[]{:S(2)}) async-start(bf16[64,2,640]{2,1,0:T(2,128)(2,1)} %reshape.52), calls=%async_computation.4 | async-start | bytes 327680 | tf_op jit(solution)/shard_map/all_to_all | solution.py:97
Sparse Core Ops, SparseCore 0:
  9.5 46.3 all-gather.5
  153.5 25.2 all-gather.3
where the time goes:
time: 235 us; the launch traced here: 234 us
  waiting for transfers between devices  104 us (44%)
  starting transfers between devices  50.9 us (22%)
  blocking collectives  37.9 us (16%)
  local copies, waits for them, and re-layouts  18 us (8%)
  between operations  13.6 us (6%)
  matrix products  9.05 us (4%)
    all_gather x1, waiting for transfers between devices, on_device(): value_blocks = lax.all_gather(w_value_out, 'ey', axis=0, tiled=False)  28.6 us
    psum x1, blocking collectives, on_device(): column_sums = lax.psum(column_terms, 'head')  25.1 us
    all_gather x1, waiting for transfers between devices, on_device(): flat_rows = lax.all_gather(arrived_cols, 'head', axis=1, tiled=True)  19.3 us
    all_to_all x1, waiting for transfers between devices, on_device(): lax.all_to_all(summed_rows, EXPERT, split_axis=0, concat_axis=0, tiled=True)  18.2 us
    all_to_all x1, starting transfers between devices, on_device(): lax.all_to_all(latent_copies, 'ez', split_axis=0, concat_axis=0, tiled=True)  15.2 us
    all_to_all x1, waiting for transfers between devices, on_device(): lax.all_to_all(outgoing, EXPERT, split_axis=0, concat_axis=0, tiled=True)  14.4 us
    all_to_all x1, starting transfers between devices, on_device(): lax.all_to_all(summed_rows, EXPERT, split_axis=0, concat_axis=0, tiled=True)  13.5 us
    all_gather x1, blocking collectives, on_device(): hidden_all = lax.all_gather(hidden, 'head', axis=1, tiled=True)  12.8 us
  transfers between devices with their start and end apart: 7, of which 6 were waited for; matrix products, arithmetic and copies ran while one was open for 9% of the time, Pallas kernels for 0%

commit v1 on v0

--- a/solution.py
+++ b/solution.py
@@ -51,8 +51,14 @@
         "sk,jkc->sjc", gathered, value_blocks, preferred_element_type=jnp.float32
     ).reshape(gathered.shape[0], -1)
     column_sums = lax.psum(column_terms, "head")
-    attention = lax.all_to_all(
-        column_sums.astype(jnp.bfloat16), "ez", split_axis=0, concat_axis=1, tiled=True
+    attention = jnp.concatenate(
+        lax.all_to_all(
+            jnp.stack(jnp.split(column_sums.astype(jnp.bfloat16), lax.axis_size("ez"), axis=0)),
+            "ez",
+            0,
+            0,
+        ),
+        axis=1,
     )
     stream = resid.astype(jnp.float32) + attention.astype(jnp.float32)
     mean_square = jnp.mean(stream * stream, axis=1, keepdims=True)

time: 235 us -> 246 us (1.047)
  local copies, waits for them, and re-layouts: 18 us -> 28.5 us
    unnamed x13 -> x32, local copies, waits for them, and re-layouts: 1.48 us -> 10.4 us
  transfers between devices with their start and end apart: 7 -> 7, of which waited for: 6 -> 6; matrix products, arithmetic and copies ran while one was open for 9% -> 8% of each run, Pallas kernels for 0% -> 0%
where the time goes in v1:
time: 246 us; the launch traced here: 245 us
  waiting for transfers between devices  104 us (42%)
  starting transfers between devices  50.9 us (21%)
  blocking collectives  37.9 us (15%)
  local copies, waits for them, and re-layouts  28.5 us (12%)
  between operations  13.6 us (6%)
  matrix products  9.01 us (4%)
    all_gather x1, waiting for transfers between devices, on_device(): value_blocks = lax.all_gather(w_value_out, 'ey', axis=0, tiled=False)  28.6 us
    psum x1, blocking collectives, on_device(): column_sums = lax.psum(column_terms, 'head')  25.1 us
    all_gather x1, waiting for transfers between devices, on_device(): flat_rows = lax.all_gather(arrived_cols, 'head', axis=1, tiled=True)  19.3 us
    all_to_all x1, waiting for transfers between devices, on_device(): lax.all_to_all(summed_rows, EXPERT, split_axis=0, concat_axis=0, tiled=True)  18.2 us
    all_to_all x1, starting transfers between devices, on_device(): lax.all_to_all(latent_copies, 'ez', split_axis=0, concat_axis=0, tiled=True)  15.2 us
    all_to_all x1, waiting for transfers between devices, on_device(): lax.all_to_all(outgoing, EXPERT, split_axis=0, concat_axis=0, tiled=True)  14.4 us
    all_to_all x1, starting transfers between devices, on_device(): lax.all_to_all(summed_rows, EXPERT, split_axis=0, concat_axis=0, tiled=True)  13.5 us
    all_gather x1, blocking collectives, on_device(): hidden_all = lax.all_gather(hidden, 'head', axis=1, tiled=True)  12.8 us
  transfers between devices with their start and end apart: 7, of which 6 were waited for; matrix products, arithmetic and copies ran while one was open for 8% of the time, Pallas kernels for 0%

profile of v1, /device:TPU:8, one launch (start us, length us, event | category | flops | bytes accessed | tf_op | source)
XLA Modules:
  0.0 244.7 jit_solution(16344329318623246016)
XLA Ops:
  6.5 0.7 all-gather.6.cloned.1.call-update
  7.3 1.6 fusion.20
  8.9 1.1 fusion.8
  10.5 1.1 broadcast_in_dim.33
  11.6 15.2 %all-to-all-start = ((bf16[16,8,4096]{2,1,0:T(8,128)(2,1)}), bf16[16,8,4096]{2,1,0:T(8,128)(2,1)S(1)}, u32[]{:S(2)}, u32[]{:S(2)}) async-start(bf16[16,8,4096]{2,1,0:T(8,128)(2,1)} %broadcast_in_dim.33), calls=%async_computation | async-start | bytes 2097152 | tf_op jit(solution)/shard_map/all_to_all | solution.py:47
  27.3 28.6 %all-gather.6.cloned.1.call-done = bf16[16384,80]{0,1:T(8,128)(2,1)} async-done(((bf16[4096,80]{0,1:T(8,128)(2,1)}), bf16[16384,80]{0,1:T(8,128)(2,1)}) %all-gather.6.cloned.1.call-update) | async-done | bytes 2621456 | tf_op jit(solution)/shard_map/all_gather | solution.py:49
  55.9 5.5 %reshape.54 = bf16[4,4096,80]{1,0,2:T(4,128)(2,1)} reshape(bf16[16384,80]{0,1:T(8,128)(2,1)} %all-gather.6.cloned.1.call-done) | data formatting | bytes 5242880 | tf_op jit(solution)/shard_map/all_gather | solution.py:49
  61.4 4.7 %copy.37 = bf16[4,80,4096]{2,1,0:T(8,128)(2,1)} copy(bf16[4,80,4096]{2,0,1:T(4,128)(2,1)} %bitcast.81) | data formatting | bytes 5242880 | tf_op jit(solution)/shard_map/sk,jkc->sjc/dot_general | solution.py:50
  66.1 10.7 %all-to-all-done = bf16[16,8,4096]{2,1,0:T(8,128)(2,1)S(1)} async-done(((bf16[16,8,4096]{2,1,0:T(8,128)(2,1)}), bf16[16,8,4096]{2,1,0:T(8,128)(2,1)S(1)}, u32[]{:S(2)}, u32[]{:S(2)}) %all-to-all-start) | async-done | bytes 1048608 | tf_op jit(solution)/shard_map/all_to_all | solution.py:47
  76.8 2.6 %fusion.9 = f32[128,320]{0,1:T(8,128)S(1)} fusion(bf16[320,4096]{1,0:T(8,128)(2,1)} %bitcast.80, bf16[16,8,4096]{2,1,0:T(8,128)(2,1)S(1)} %all-to-all-done), kind=kOutput, calls=%fused_computation.14 | convolution fusion | flops 335544320 | bytes 3833856 | tf_op jit(solution)/shard_map/sk,jkc->sjc/dot_general | solution.py:50
  79.4 25.1 %all-reduce.1 = bf16[128,320]{0,1:T(8,128)(2,1)S(1)} all-reduce(f32[128,320]{0,1:T(8,128)S(1)} %fusion.9), channel_id=1, replica_groups=mesh['head'=8,'ez'=16,'ey'=4] {'head'}, use_global_device_ids=true, to_apply=%region_2.3 | all-reduce | flops 40960 | bytes 245760 | tf_op jit(solution)/shard_map/psum | solution.py:53
  106.2 0.6 constant_dynamic-update-slice_fusion.15
  108.6 0.6 constant_dynamic-update-slice_fusion.11
  109.8 0.6 constant_dynamic-update-slice_fusion.9
  114.6 0.6 constant_dynamic-update-slice_fusion.1
  115.7 10.2 %all-to-all-start.1 = ((bf16[16,8,320]{2,1,0:T(8,128)(2,1)}), bf16[16,8,320]{2,1,0:T(8,128)(2,1)S(1)}, u32[]{:S(2)}, u32[]{:S(2)}) async-start(bf16[16,8,320]{2,1,0:T(8,128)(2,1)} %constant_dynamic-update-slice_fusion), calls=%async_computation.1 | async-start | bytes 196608 | tf_op jit(solution)/shard_map/all_to_all | solution.py:55
  126.1 0.8 dynamic-slice
  126.9 12.1 %all-to-all-done.1 = bf16[16,8,320]{2,1,0:T(8,128)(2,1)S(1)} async-done(((bf16[16,8,320]{2,1,0:T(8,128)(2,1)}), bf16[16,8,320]{2,1,0:T(8,128)(2,1)S(1)}, u32[]{:S(2)}, u32[]{:S(2)}) %all-to-all-start.1) | async-done | bytes 81952 | tf_op jit(solution)/shard_map/all_to_all | solution.py:55
  139.6 0.7 reshape.48
  140.4 7.0 %all-to-all-start.2 = ((bf16[64,2,640]{2,1,0:T(2,128)(2,1)}), bf16[64,2,640]{2,1,0:T(2,128)(2,1)S(1)}, u32[]{:S(2)}, u32[]{:S(2)}) async-start(bf16[64,2,640]{2,1,0:T(2,128)(2,1)} %reshape.48), calls=%async_computation.2 | async-start | bytes 327680 | tf_op jit(solution)/shard_map/all_to_all | solution.py:88
  147.4 1.3 copy.59
  148.7 14.4 %all-to-all-done.2 = bf16[64,2,640]{2,1,0:T(2,128)(2,1)S(1)} async-done(((bf16[64,2,640]{2,1,0:T(2,128)(2,1)}), bf16[64,2,640]{2,1,0:T(2,128)(2,1)S(1)}, u32[]{:S(2)}, u32[]{:S(2)}) %all-to-all-start.2) | async-done | bytes 163872 | tf_op jit(solution)/shard_map/all_to_all | solution.py:88
  163.1 0.7 reshape.49
  163.8 1.1 copy.57
  164.9 5.0 %all-to-all-start.3 = ((bf16[96,8,640]{2,0,1:T(8,128)(2,1)}), bf16[96,8,640]{2,0,1:T(8,128)(2,1)S(1)}, u32[]{:S(2)}, u32[]{:S(2)}) async-start(bf16[96,8,640]{2,0,1:T(8,128)(2,1)} %copy.57), calls=%async_computation.3 | async-start | bytes 1966080 | tf_op jit(solution)/shard_map/all_to_all | solution.py:93
  169.9 19.3 %all-gather.4.cloned.1.call-done = bf16[128,5120]{1,0:T(8,128)(2,1)} async-done(((bf16[128,640]{1,0:T(8,128)(2,1)}), bf16[128,5120]{1,0:T(8,128)(2,1)}) %all-gather.4.cloned.1.call-update) | async-done | bytes 1310736 | tf_op jit(solution)/shard_map/all_gather | solution.py:95
  189.2 2.0 fusion.1
  191.3 12.8 %all_gather.15 = bf16[128,768]{0,1:T(8,128)(2,1)S(1)} all-gather(bf16[128,96]{0,1:T(8,128)(2,1)S(1)} %fusion.12), channel_id=1, replica_groups=mesh['head'=8,'ez'=16,'ey'=4] {'head'}, dimensions={1}, use_global_device_ids=true | all-gather | bytes 221184 | tf_op jit(solution)/shard_map/all_gather | solution.py:98
  204.4 0.7 reshape.51
  205.1 13.5 %all-to-all-start.4 = ((bf16[64,2,640]{2,1,0:T(2,128)(2,1)}), bf16[64,2,640]{2,1,0:T(2,128)(2,1)S(1)}, u32[]{:S(2)}, u32[]{:S(2)}) async-start(bf16[64,2,640]{2,1,0:T(2,128)(2,1)} %reshape.51), calls=%async_computation.4 | async-start | bytes 327680 | tf_op jit(solution)/shard_map/all_to_all | solution.py:103
  218.8 18.2 %all-to-all-done.4 = bf16[64,2,640]{2,1,0:T(2,128)(2,1)S(1)} async-done(((bf16[64,2,640]{2,1,0:T(2,128)(2,1)}), bf16[64,2,640]{2,1,0:T(2,128)(2,1)S(1)}, u32[]{:S(2)}, u32[]{:S(2)}) %all-to-all-start.4) | async-done | bytes 163872 | tf_op jit(solution)/shard_map/all_to_all | solution.py:103
  237.1 0.8 convolution_add_fusion.1
  (69 shorter events, 11.3 us)
Async XLA Ops:
  6.5 182.7 %copy-start = (bf16[1,2,96,5120]{3,2,1,0:T(8,128)(2,1)S(1)}, bf16[1,2,96,5120]{3,2,1,0:T(8,128)(2,1)}, u32[]{:S(2)}) copy-start(bf16[1,2,96,5120]{3,2,1,0:T(8,128)(2,1)} %param.22) | copy-start | bytes 5898244
  6.5 3.6 %copy-start.1 = (bf16[8,128,512]{2,1,0:T(8,128)(2,1)S(1)}, bf16[8,128,512]{2,1,0:T(8,128)(2,1)}, u32[]{:S(2)}) copy-start(bf16[8,128,512]{2,1,0:T(8,128)(2,1)} %param.14) | copy-start | bytes 3145732
  6.5 49.3 %all-gather.6.cloned.1.call-start = ((), (), s32[]{:S(2)}) async-start(), calls=%async_computation.6 | async-start | bytes 3276800 | tf_op jit(solution)/shard_map/all_gather | solution.py:49
  10.4 16.4 %copy-start.5 = (s32[8,6]{1,0:T(8,128)S(1)}, s32[8,6]{1,0:T(8,128)}, u32[]{:S(2)}) copy-start(s32[8,6]{1,0:T(8,128)} %param.20) | copy-start | bytes 580
  11.6 65.2 %all-to-all-start = ((bf16[16,8,4096]{2,1,0:T(8,128)(2,1)}), bf16[16,8,4096]{2,1,0:T(8,128)(2,1)S(1)}, u32[]{:S(2)}, u32[]{:S(2)}) async-start(bf16[16,8,4096]{2,1,0:T(8,128)(2,1)} %broadcast_in_dim.33), calls=%async_computation | async-start | bytes 2097152 | tf_op jit(solution)/shard_map/all_to_all | solution.py:47
  104.9 34.3 %copy-start.2 = (bf16[8,5120]{1,0:T(8,128)(2,1)S(1)}, bf16[8,5120]{1,0:T(8,128)(2,1)}, u32[]{:S(2)}) copy-start(bf16[8,5120]{1,0:T(8,128)(2,1)} %param.18) | copy-start | bytes 245764
  115.7 23.2 %all-to-all-start.1 = ((bf16[16,8,320]{2,1,0:T(8,128)(2,1)}), bf16[16,8,320]{2,1,0:T(8,128)(2,1)S(1)}, u32[]{:S(2)}, u32[]{:S(2)}) async-start(bf16[16,8,320]{2,1,0:T(8,128)(2,1)} %constant_dynamic-update-slice_fusion), calls=%async_computation.1 | async-start | bytes 196608 | tf_op jit(solution)/shard_map/all_to_all | solution.py:55
  126.1 12.9 %copy-start.3 = (s32[8,6]{0,1:T(8,128)}, s32[8,6]{0,1:T(8,128)S(1)}, u32[]{:S(2)}) copy-start(s32[8,6]{0,1:T(8,128)S(1)} %copy.55) | copy-start | bytes 580
  140.4 22.7 %all-to-all-start.2 = ((bf16[64,2,640]{2,1,0:T(2,128)(2,1)}), bf16[64,2,640]{2,1,0:T(2,128)(2,1)S(1)}, u32[]{:S(2)}, u32[]{:S(2)}) async-start(bf16[64,2,640]{2,1,0:T(2,128)(2,1)} %reshape.48), calls=%async_computation.2 | async-start | bytes 327680 | tf_op jit(solution)/shard_map/all_to_all | solution.py:88
  147.3 41.9 %all-gather.4.cloned.1.call-start = ((), (), s32[]{:S(2)}) async-start(), calls=%async_computation.5 | async-start | bytes 1474560 | tf_op jit(solution)/shard_map/all_gather | solution.py:95
  164.9 39.1 %all-to-all-start.3 = ((bf16[96,8,640]{2,0,1:T(8,128)(2,1)}), bf16[96,8,640]{2,0,1:T(8,128)(2,1)S(1)}, u32[]{:S(2)}, u32[]{:S(2)}) async-start(bf16[96,8,640]{2,0,1:T(8,128)(2,1)} %copy.57), calls=%async_computation.3 | async-start | bytes 1966080 | tf_op jit(solution)/shard_map/all_to_all | solution.py:93
  191.2 27.4 %copy-start.6 = (f32[8,6]{1,0:T(8,128)S(1)}, f32[8,6]{1,0:T(8,128)}, u32[]{:S(2)}) copy-start(f32[8,6]{1,0:T(8,128)} %param.21) | copy-start | bytes 580
  191.2 27.5 %copy-start.4 = (s32[8,6]{0,1:T(8,128)S(1)}, s32[8,6]{0,1:T(8,128)}, u32[]{:S(2)}) copy-start(s32[8,6]{0,1:T(8,128)} %copy-done.3) | copy-start | bytes 580
  205.1 31.9 %all-to-all-start.4 = ((bf16[64,2,640]{2,1,0:T(2,128)(2,1)}), bf16[64,2,640]{2,1,0:T(2,128)(2,1)S(1)}, u32[]{:S(2)}, u32[]{:S(2)}) async-start(bf16[64,2,640]{2,1,0:T(2,128)(2,1)} %reshape.51), calls=%async_computation.4 | async-start | bytes 327680 | tf_op jit(solution)/shard_map/all_to_all | solution.py:103
Sparse Core Ops, SparseCore 0:
  9.5 46.3 all-gather.5
  164.0 25.2 all-gather.3
